TPU v7x, 256 devices: a whole 4x4x8 slice. The times are simulated.
256 devices in a mesh: expert: 64 (over y, z, core), tensor: 4 (over x).
Axes of the slice: x: 4, y: 4, z: 8, core: 2. Of those that a mesh axis runs over, the one named last changes fastest.
Arguments:
- tokens: bfloat16 [8192, 2048], P('expert', 'tensor'), may hold values from -6 to 6
- labels: int32 [8192, 1], P('expert'), may hold values from 0 to 31, as said below
- domain_ids: int32 [8192], P('expert'), may hold values from 0 to 21
- domain_weights: float32 [22], replicated, may hold values from 0.02 to 0.5
- cotangent: bfloat16 [8192, 2048], P('expert', 'tensor'), may hold values from -6 to 6
- gate_weight: bfloat16 [64, 2048, 2048], P('expert', None, 'tensor'), may hold values from -0.125 to 0.125
- up_weight: bfloat16 [64, 2048, 2048], P('expert', None, 'tensor'), may hold values from -0.125 to 0.125
- down_weight: bfloat16 [64, 2048, 2048], P('expert', 'tensor'), may hold values from -0.09375 to 0.09375
Outputs:
- layer_out: bfloat16 [8192, 2048], P('expert', 'tensor')
- input_grad: bfloat16 [8192, 2048], P('expert', 'tensor')
- gate_grad: bfloat16 [64, 2048, 2048], P('expert', None, 'tensor')
- up_grad: bfloat16 [64, 2048, 2048], P('expert', None, 'tensor')
- down_grad: bfloat16 [64, 2048, 2048], P('expert', 'tensor')
Inputs may be any that keep to these rules, and one draw needn't show every extreme that they name: `labels`: among the rows of one device (aligned blocks of 128 rows) no label appears more than 8 times, and every such block has some label exactly 8 times.
All inputs are finite; a program needn't handle non-finite values.
Results may differ from a plain program's by a relative error of at most 0.0058.
Values may be sent and summed in bfloat16 or wider, within the bound.
No kernel may reach another device: no remote copies, remote signals or barrier semaphores. Data moves between devices by JAX's collectives and lax.ppermute only.
A program may use at most 320 MiB of HBM per device.

v0:
```python
import jax
import jax.numpy as jnp
from jax import lax
from jax.sharding import PartitionSpec as P

SPLIT = 2


def partner(value, axis, stride):
    return lax.ppermute(value, axis, [(i, i ^ 1 << stride) for i in range(lax.axis_size(axis))])


def silu_parts(gate_pre):
    squash = jax.nn.sigmoid(gate_pre)
    return (squash, gate_pre * squash)


def body(
    tokens, labels, domain_ids, domain_weights, cotangent, gate_weight, up_weight, down_weight
):
    n_expert = lax.axis_size("expert")
    tok_rows = tokens.shape[0]
    experts_all = n_expert // SPLIT
    capacity = 2 * tok_rows // experts_all
    half_cap = capacity // 2
    parity = lax.axis_index("expert") % 2
    lang_label = labels[:, 0]
    dom_hot = (
        domain_ids[:, None] == jnp.arange(domain_weights.shape[0], dtype=jnp.int32)[None, :]
    ).astype(jnp.float32)
    tok_scale = jnp.sum(dom_hot * domain_weights[None, :], axis=1)
    grad_rows = (tok_scale[:, None] * cotangent.astype(jnp.float32)).astype(jnp.bfloat16)
    lab_hot = (lang_label[:, None] == jnp.arange(experts_all, dtype=jnp.int32)[None, :]).astype(
        jnp.float32
    )
    row_ids = jnp.arange(tok_rows, dtype=jnp.int32)
    earlier = (row_ids[None, :] < row_ids[:, None]).astype(jnp.float32)
    before = jnp.dot(earlier, lab_hot, precision=lax.Precision.HIGHEST)
    slot_pos = jnp.sum(before * lab_hot, axis=1).astype(jnp.int32)
    target_row = lang_label * capacity + slot_pos
    sources = jnp.stack((tokens, grad_rows))
    sources = lax.all_gather(sources, "tensor", axis=2, tiled=True)
    slot_ids = jnp.arange(n_expert * capacity, dtype=jnp.int32)
    dispatch_map = (slot_ids[:, None] // capacity // SPLIT == lang_label[None, :]) & (
        slot_ids[:, None] % capacity == slot_pos[None, :]
    )
    dispatch_map = dispatch_map.astype(jnp.bfloat16)
    outbound = jnp.einsum(
        "rt,ktw->krw", dispatch_map, sources, preferred_element_type=jnp.float32
    ).astype(jnp.bfloat16)
    outbound = outbound.reshape(2, n_expert, capacity, sources.shape[2])
    arrived = lax.all_to_all(outbound, "expert", split_axis=1, concat_axis=1, tiled=True)
    rows_all = n_expert * capacity
    feat_width = arrived.shape[3]
    routed = arrived[0].reshape(rows_all, feat_width)
    routed_grad = arrived[1].reshape(rows_all, feat_width)
    w_gate = gate_weight[0]
    w_up = up_weight[0]
    w_down = down_weight[0]
    contract_rows = (((0,), (0,)), ((), ()))
    contract_cols = (((1,), (1,)), ((), ()))
    gate_pre = jnp.dot(routed, w_gate, preferred_element_type=jnp.float32)
    up_pre = jnp.dot(routed, w_up, preferred_element_type=jnp.float32)
    squash, activated = silu_parts(gate_pre)
    hidden = (activated * up_pre).astype(jnp.bfloat16)
    out_part = jnp.dot(hidden, w_down, preferred_element_type=jnp.float32)
    grad_hidden = lax.dot_general(
        routed_grad, w_down, contract_cols, preferred_element_type=jnp.float32
    )
    grad_gate_pre = (grad_hidden * up_pre * squash * (1.0 + gate_pre * (1.0 - squash))).astype(
        jnp.bfloat16
    )
    grad_up_pre = (grad_hidden * activated).astype(jnp.bfloat16)
    gate_grad = lax.dot_general(
        routed, grad_gate_pre, contract_rows, preferred_element_type=jnp.float32
    ).astype(jnp.bfloat16)[None]
    up_grad = lax.dot_general(
        routed, grad_up_pre, contract_rows, preferred_element_type=jnp.float32
    ).astype(jnp.bfloat16)[None]
    down_grad = lax.dot_general(
        hidden, routed_grad, contract_rows, preferred_element_type=jnp.float32
    ).astype(jnp.bfloat16)[None]
    input_part = lax.dot_general(
        grad_gate_pre, w_gate, contract_cols, preferred_element_type=jnp.float32
    ) + lax.dot_general(grad_up_pre, w_up, contract_cols, preferred_element_type=jnp.float32)
    out_part = out_part.reshape(n_expert, capacity, feat_width)
    input_part = input_part.reshape(n_expert, capacity, feat_width)
    out_share, input_share = (
        lax.psum_scatter(out_part, "tensor", scatter_dimension=2, tiled=True),
        lax.psum_scatter(input_part, "tensor", scatter_dimension=2, tiled=True),
    )
    partial_value = jnp.stack((out_share, input_share))
    kept = jnp.where(parity == 0, partial_value[:, :, :half_cap], partial_value[:, :, half_cap:])
    handed = jnp.where(parity == 0, partial_value[:, :, half_cap:], partial_value[:, :, :half_cap])
    summed = kept + partner(handed, "expert", 0)
    going_back = summed.astype(jnp.bfloat16)
    returned = lax.all_to_all(going_back, "expert", split_axis=1, concat_axis=1, tiled=True)
    home_ids = jnp.arange(n_expert * half_cap, dtype=jnp.int32)
    home_map = (home_ids[:, None] == target_row[None, :]).astype(jnp.bfloat16)
    flat_back = returned.reshape(2, n_expert * half_cap, returned.shape[3])
    gathered_home = jnp.einsum(
        "rt,krw->ktw", home_map, flat_back, preferred_element_type=jnp.float32
    ).astype(jnp.bfloat16)
    return (gathered_home[0], gathered_home[1], gate_grad, up_grad, down_grad)


def solution(mesh):
    return jax.shard_map(
        body,
        mesh=mesh,
        in_specs=(
            P("expert", "tensor"),
            P("expert", None),
            P("expert"),
            P(),
            P("expert", "tensor"),
            P("expert", None, "tensor"),
            P("expert", None, "tensor"),
            P("expert", "tensor", None),
        ),
        out_specs=(
            P("expert", "tensor"),
            P("expert", "tensor"),
            P("expert", None, "tensor"),
            P("expert", None, "tensor"),
            P("expert", "tensor", None),
        ),
        check_vma=False,
    )
```

profile of v0, /device:TPU:1, one launch (start us, length us, event | category | flops | bytes accessed | tf_op | source)
XLA Modules:
  0.0 302.7 jit_solution(17173675187760145169)
XLA Ops:
  7.2 0.0 copy-start
  7.2 0.0 all-gather.2.cloned.1.call-start
  7.2 0.9 select_reduce_fusion
  8.1 1.0 fusion.24
  9.1 1.6 pad_maximum_fusion.1
  10.8 0.0 all-gather.2.cloned.1.call-update
  10.8 0.0 reduce-scatter.5.cloned.1.call-start
  10.8 0.9 fusion.15
  11.7 28.7 %all-gather.2.cloned.1.call-done = bf16[2,128,2048]{2,1,0:T(8,128)(2,1)} async-done(((bf16[2,128,512]{2,1,0:T(8,128)(2,1)}), bf16[2,128,2048]{2,1,0:T(8,128)(2,1)}) %all-gather.2.cloned.1.call-update) | async-done | bytes 1048592 | tf_op jit(solution)/shard_map/all_gather | solution.py:42
  40.4 2.5 convert_bitcast_fusion
  42.9 0.6 copy.27
  43.5 0.0 copy-start.6
  43.5 107.7 %all_to_all.10 = bf16[2,64,8,2048]{3,2,0,1:T(8,128)(2,1)S(1)} all-to-all(bf16[2,64,8,2048]{3,2,0,1:T(8,128)(2,1)S(1)} %copy.27), channel_id=1, replica_groups=mesh['expert'=64,'tensor'=4] {'expert'}, dimensions={1} | all-to-all | bytes 8388608 | tf_op jit(solution)/shard_map/all_to_all | solution.py:52
  151.2 0.0 copy-done.6
  151.3 1.2 fusion.12
  152.5 1.9 copy-done.5
  154.4 1.3 fusion.5
  155.6 0.0 copy-done.1
  155.7 1.6 multiply_convert_fusion.2
  157.3 0.0 copy-start.7
  157.3 0.0 copy-start.9
  157.3 1.3 fusion.10
  158.6 0.0 copy-done.7
  158.6 0.0 copy-done.10
  158.7 3.3 %add_bitcast_fusion = f32[64,8,2048]{2,1,0:T(8,128)} fusion(f32[512,2048]{1,0:T(8,128)S(1)} %fusion.10, bf16[512,512]{1,0:T(8,128)(2,1)S(1)} %get-tuple-element.27, bf16[1,2048,512]{2,1,0:T(8,128)(2,1)S(1)} %copy-done), kind=kOutput, calls=%fused_computation | convolution fusion | flops 1074790400 | bytes 11010048 | tf_op jit(solution)/shard_map/dot_general | solution.py:85
  161.9 0.0 reduce-scatter.5.cloned.1.call-update
  161.9 0.0 reduce-scatter.3.cloned.1.call-start
  162.0 4.8 %fusion.3 = f32[64,8,2048]{2,1,0:T(8,128)} fusion(bf16[1,512,2048]{2,1,0:T(8,128)(2,1)} %param.15, bf16[512,512]{1,0:T(8,128)(2,1)S(1)} %get-tuple-element.25), kind=kOutput, calls=%fused_computation.12 | convolution fusion | flops 1073741824 | bytes 6815744 | tf_op jit(solution)/shard_map/dot_general | solution.py:66
  166.8 0.0 reduce-scatter.3.cloned.1.call-update
  166.9 40.1 %reduce-scatter.5.cloned.1.call-done = f32[64,8,512]{2,1,0:T(8,128)} async-done(((f32[64,8,2048]{2,1,0:T(8,128)}), f32[64,8,512]{2,1,0:T(8,128)}) %reduce-scatter.5.cloned.1.call-update) | async-done | bytes 1048592 | tf_op jit(solution)/shard_map/reduce_scatter | solution.py:90
  207.0 51.8 %reduce-scatter.3.cloned.1.call-done = f32[64,8,512]{2,1,0:T(8,128)} async-done(((f32[64,8,2048]{2,1,0:T(8,128)}), f32[64,8,512]{2,1,0:T(8,128)}) %reduce-scatter.3.cloned.1.call-update) | async-done | bytes 1048592 | tf_op jit(solution)/shard_map/reduce_scatter | solution.py:89
  258.8 2.8 broadcast_select_fusion
  261.6 0.0 copy-start.12
  261.7 0.7 collective-permute-start
  262.4 2.3 collective-permute-done
  264.7 0.4 add_convert_fusion
  265.1 1.0 copy.28
  266.1 10.4 %all-to-all-start.1 = ((bf16[2,64,4,512]{3,2,0,1:T(4,128)(2,1)}), bf16[2,64,4,512]{3,2,0,1:T(4,128)(2,1)S(1)}, u32[]{:S(2)}, u32[]{:S(2)}) async-start(bf16[2,64,4,512]{3,2,0,1:T(4,128)(2,1)} %copy.28), calls=%async_computation.3 | async-start | bytes 1048576 | tf_op jit(solution)/shard_map/all_to_all | solution.py:97
  276.5 0.0 copy-start.8
  276.5 4.5 %fusion.2 = bf16[1,512,2048]{2,1,0:T(8,128)(2,1)} fusion(bf16[512,512]{1,0:T(8,128)(2,1)} %copy-done.9, bf16[2,64,8,2048]{3,2,0,1:T(8,128)(2,1)} %copy-done.1), kind=kOutput, calls=%fused_computation.7 | convolution fusion | flops 1074790400 | bytes 4718592 | tf_op jit(solution)/shard_map/dot_general | solution.py:80
  281.0 0.0 copy-done.8
  281.0 2.6 fusion
  283.7 2.6 fusion.1
  286.3 7.5 %all-to-all-done.1 = bf16[2,64,4,512]{3,2,0,1:T(4,128)(2,1)S(1)} async-done(((bf16[2,64,4,512]{3,2,0,1:T(4,128)(2,1)}), bf16[2,64,4,512]{3,2,0,1:T(4,128)(2,1)S(1)}, u32[]{:S(2)}, u32[]{:S(2)}) %all-to-all-start.1) | async-done | bytes 524320 | tf_op jit(solution)/shard_map/all_to_all | solution.py:97
  293.8 0.4 copy.29
  294.2 0.3 fusion.14
  294.6 0.8 copy.31
  295.4 0.8 copy.32
  (18 shorter events, 0.1 us)
Async XLA Ops:
  7.2 148.5 %copy-start = (bf16[1,2048,512]{2,1,0:T(8,128)(2,1)S(1)}, bf16[1,2048,512]{2,1,0:T(8,128)(2,1)}, u32[]{:S(2)}) copy-start(bf16[1,2048,512]{2,1,0:T(8,128)(2,1)} %param.14) | copy-start | bytes 6291460
  7.2 33.2 %all-gather.2.cloned.1.call-start = ((), (), s32[]{:S(2)}) async-start(), calls=%async_computation.4 | async-start | bytes 1310720 | tf_op jit(solution)/shard_map/all_gather | solution.py:42
  10.8 196.2 %reduce-scatter.5.cloned.1.call-start = ((), (), s32[]{:S(2)}) async-start(), calls=%async_computation.6 | async-start | bytes 5242880 | tf_op jit(solution)/shard_map/reduce_scatter | solution.py:90
  43.5 107.7 %copy-start.6 = (bf16[1,2048,512]{2,1,0:T(8,128)(2,1)S(1)}, bf16[1,2048,512]{2,1,0:T(8,128)(2,1)}, u32[]{:S(2)}) copy-start(bf16[1,2048,512]{2,1,0:T(8,128)(2,1)} %param.13) | copy-start | bytes 6291460
  151.2 4.4 %copy-start.1 = (bf16[2,64,8,2048]{3,2,0,1:T(8,128)(2,1)}, bf16[2,64,8,2048]{3,2,0,1:T(8,128)(2,1)S(1)}, u32[]{:S(2)}) copy-start(bf16[2,64,8,2048]{3,2,0,1:T(8,128)(2,1)S(1)} %all_to_all.10) | copy-start | bytes 12582916
  151.2 3.1 %copy-start.5 = (bf16[1,512,2048]{2,1,0:T(8,128)(2,1)S(1)}, bf16[1,512,2048]{2,1,0:T(8,128)(2,1)}, u32[]{:S(2)}) copy-start(bf16[1,512,2048]{2,1,0:T(8,128)(2,1)} %param.15) | copy-start | bytes 6291460
  157.3 1.3 copy-start.7
  157.3 1.3 copy-start.10
  157.3 4.7 %copy-start.9 = (bf16[512,512]{1,0:T(8,128)(2,1)}, bf16[512,512]{1,0:T(8,128)(2,1)S(1)}, u32[]{:S(2)}) copy-start(bf16[512,512]{1,0:T(8,128)(2,1)S(1)} %get-tuple-element.25) | copy-start | bytes 1572868
  161.9 96.9 %reduce-scatter.3.cloned.1.call-start = ((), (), s32[]{:S(2)}) async-start(), calls=%async_computation.5 | async-start | bytes 5242880 | tf_op jit(solution)/shard_map/reduce_scatter | solution.py:89
  207.0 57.7 %copy-start.3 = (f32[64,8,512]{2,1,0:T(8,128)S(1)}, f32[64,8,512]{2,1,0:T(8,128)}, u32[]{:S(2)}) copy-start(f32[64,8,512]{2,1,0:T(8,128)} %reduce-scatter.5.cloned.1.call-done) | copy-start | bytes 3145732
  258.8 5.8 %copy-start.4 = (f32[64,8,512]{2,1,0:T(8,128)S(1)}, f32[64,8,512]{2,1,0:T(8,128)}, u32[]{:S(2)}) copy-start(f32[64,8,512]{2,1,0:T(8,128)} %reduce-scatter.3.cloned.1.call-done) | copy-start | bytes 3145732
  261.6 14.8 %copy-start.12 = (s32[128,1]{0,1:T(1,128)S(1)}, s32[128,1]{0,1:T(1,128)}, u32[]{:S(2)}) copy-start(s32[128,1]{0,1:T(1,128)} %param.9) | copy-start | bytes 1540
  261.7 3.0 collective-permute-start
  266.1 27.7 %all-to-all-start.1 = ((bf16[2,64,4,512]{3,2,0,1:T(4,128)(2,1)}), bf16[2,64,4,512]{3,2,0,1:T(4,128)(2,1)S(1)}, u32[]{:S(2)}, u32[]{:S(2)}) async-start(bf16[2,64,4,512]{3,2,0,1:T(4,128)(2,1)} %copy.28), calls=%async_computation.3 | async-start | bytes 1048576 | tf_op jit(solution)/shard_map/all_to_all | solution.py:97
  276.5 4.5 %copy-start.2 = (bf16[2,64,8,2048]{3,2,0,1:T(8,128)(2,1)S(1)}, bf16[2,64,8,2048]{3,2,0,1:T(8,128)(2,1)}, u32[]{:S(2)}) copy-start(bf16[2,64,8,2048]{3,2,0,1:T(8,128)(2,1)} %copy-done.1) | copy-start | bytes 12582916
  276.5 4.5 %copy-start.8 = (bf16[512,512]{1,0:T(8,128)(2,1)S(1)}, bf16[512,512]{1,0:T(8,128)(2,1)}, u32[]{:S(2)}) copy-start(bf16[512,512]{1,0:T(8,128)(2,1)} %copy-done.7) | copy-start | bytes 1572868
  281.0 2.6 copy-start.11
Sparse Core Ops, SparseCore 0:
  10.9 29.4 all-gather.1
  162.1 44.8 reduce-scatter.4
  209.7 49.0 reduce-scatter.2
where the time goes:
time: 303 us
  waiting for transfers between devices  130 us (43%)
  blocking collectives  108 us (36%)
  matrix products  27 us (9%)
  between operations  14 us (5%)
  starting transfers between devices  11.2 us (4%)
  other arithmetic  6.76 us (2%)
  local copies, waits for them, and re-layouts  5.46 us (2%)
    all_to_all x1, blocking collectives, body(): lax.all_to_all(outbound, 'expert', split_axis=1, concat_axis=1, tiled=True)  108 us
    reduce_scatter x1, waiting for transfers between devices, body(): lax.psum_scatter(out_part, 'tensor', scatter_dimension=2, tiled=True)  51.8 us
    reduce_scatter x1, waiting for transfers between devices, body(): lax.psum_scatter(input_part, 'tensor', scatter_dimension=2, tiled=True)  40.1 us
    all_gather x1, waiting for transfers between devices, body(): sources = lax.all_gather(sources, 'tensor', axis=2, tiled=True)  28.7 us
    all_to_all x1, starting transfers between devices, body(): lax.all_to_all(going_back, 'expert', split_axis=1, concat_axis=1, tiled=T...  10.4 us
    all_to_all x1, waiting for transfers between devices, body(): lax.all_to_all(going_back, 'expert', split_axis=1, concat_axis=1, tiled=T...  7.52 us
  transfers between devices with their start and end apart: 5, of which 5 were waited for; matrix products, arithmetic and copies ran while one was open for 5% of the time, Pallas kernels for 0%

commit v1 on v0

--- a/solution.py
+++ b/solution.py
@@ -4,6 +4,22 @@
 from jax.sharding import PartitionSpec as P
 
 SPLIT = 2
+
+
+def ring_gather(x, axis, dim):
+    ways, here, turn = (lax.axis_size(axis), lax.axis_index(axis), x.shape[dim])
+    lengths = [n * ways if d == dim else n for d, n in enumerate(x.shape)]
+    full = lax.dynamic_update_slice_in_dim(jnp.zeros(lengths, x.dtype), x, here * turn, axis=dim)
+    going_up = going_down = x
+    for far in range(1, ways // 2 + 1):
+        going_up = lax.ppermute(going_up, axis, [(d, (d + 1) % ways) for d in range(ways)])
+        full = lax.dynamic_update_slice_in_dim(full, going_up, (here - far) % ways * turn, axis=dim)
+        if 2 * far < ways:
+            going_down = lax.ppermute(going_down, axis, [(d, (d - 1) % ways) for d in range(ways)])
+            full = lax.dynamic_update_slice_in_dim(
+                full, going_down, (here + far) % ways * turn, axis=dim
+            )
+    return full
 
 
 def partner(value, axis, stride):
@@ -39,7 +55,7 @@
     slot_pos = jnp.sum(before * lab_hot, axis=1).astype(jnp.int32)
     target_row = lang_label * capacity + slot_pos
     sources = jnp.stack((tokens, grad_rows))
-    sources = lax.all_gather(sources, "tensor", axis=2, tiled=True)
+    sources = ring_gather(sources, "tensor", 2)
     slot_ids = jnp.arange(n_expert * capacity, dtype=jnp.int32)
     dispatch_map = (slot_ids[:, None] // capacity // SPLIT == lang_label[None, :]) & (
         slot_ids[:, None] % capacity == slot_pos[None, :]

time: 303 us -> 292 us (0.964)
  waiting for transfers between devices: 130 us -> 108 us
  starting transfers between devices: 11.2 us -> 16.7 us
  blocking collectives: 108 us -> 113 us
    all_gather x1 -> x0, waiting for transfers between devices: 28.7 us -> none  [body(): sources = lax.all_gather(sources, 'tensor', axis=2, tiled=True)]
    ppermute x0 -> x3, waiting for transfers between devices: none -> 8.06 us  [the longest x2 8.05 us: ring_gather(): lax.ppermute(going_up, axis, [(d, (d + 1) % ways) for d in range(ways)])]
    ppermute x0 -> x3, starting transfers between devices: none -> 5.28 us  [the longest x2 4.01 us: ring_gather(): lax.ppermute(going_up, axis, [(d, (d + 1) % ways) for d in range(ways)])]
    all_to_all x1, blocking collectives: 108 us -> 113 us  [body(): lax.all_to_all(outbound, 'expert', split_axis=1, concat_axis=1, tiled=True)]
  transfers between devices with their start and end apart: 5 -> 7, of which waited for: 5 -> 6; matrix products, arithmetic and copies ran while one was open for 5% -> 5% of each run, Pallas kernels for 0% -> 0%
where the time goes in v1:
time: 292 us; the launch traced here: 291 us
  blocking collectives  113 us (39%)
  waiting for transfers between devices  108 us (37%)
  matrix products  25.1 us (9%)
  starting transfers between devices  16.7 us (6%)
  between operations  14.3 us (5%)
  local copies, waits for them, and re-layouts  7.53 us (3%)
  other arithmetic  6.78 us (2%)
    all_to_all x1, blocking collectives, body(): lax.all_to_all(outbound, 'expert', split_axis=1, concat_axis=1, tiled=True)  113 us
    reduce_scatter x1, waiting for transfers between devices, body(): lax.psum_scatter(out_part, 'tensor', scatter_dimension=2, tiled=True)  51.8 us
    reduce_scatter x1, waiting for transfers between devices, body(): lax.psum_scatter(input_part, 'tensor', scatter_dimension=2, tiled=True)  38.6 us
    all_to_all x1, starting transfers between devices, body(): lax.all_to_all(going_back, 'expert', split_axis=1, concat_axis=1, tiled=T...  10.4 us
    ppermute x2, waiting for transfers between devices, ring_gather(): lax.ppermute(going_up, axis, [(d, (d + 1) % ways) for d in range(ways)])  8.05 us
    all_to_all x1, waiting for transfers between devices, body(): lax.all_to_all(going_back, 'expert', split_axis=1, concat_axis=1, tiled=T...  7.53 us
  transfers between devices with their start and end apart: 7, of which 6 were waited for; matrix products, arithmetic and copies ran while one was open for 5% of the time, Pallas kernels for 0%

profile of v1, /device:TPU:1, one launch (start us, length us, event | category | flops | bytes accessed | tf_op | source)
XLA Modules:
  0.0 291.4 jit_solution(10145970223390497946)
XLA Ops:
  7.2 0.0 copy-start
  7.2 0.0 reduce-scatter.5.cloned.1.call-start
  7.2 0.9 select_reduce_fusion
  8.1 1.0 fusion.24
  9.1 0.1 broadcast_in_dim.8
  9.3 1.7 pad_maximum_fusion.1
  10.9 2.0 collective-permute-start
  13.0 1.3 collective-permute-start.1
  14.2 0.2 fusion.15
  14.4 3.8 %collective-permute-done = bf16[2,128,512]{2,1,0:T(8,128)(2,1)S(1)} collective-permute-done((bf16[2,128,512]{2,1,0:T(8,128)(2,1)}, bf16[2,128,512]{2,1,0:T(8,128)(2,1)S(1)}, u32[]{:S(2)}, u32[]{:S(2)}) %collective-permute-start) | collective-permute-done | bytes 262176 | tf_op jit(solution)/shard_map/ppermute | solution.py:15
  18.2 2.0 collective-permute-start.2
  20.2 0.0 collective-permute-done.1
  20.2 1.0 constant_dynamic-update-slice_fusion.1
  21.2 4.2 %collective-permute-done.2 = bf16[2,128,512]{2,1,0:T(8,128)(2,1)} collective-permute-done((bf16[2,128,512]{2,1,0:T(8,128)(2,1)S(1)}, bf16[2,128,512]{2,1,0:T(8,128)(2,1)}, u32[]{:S(2)}, u32[]{:S(2)}) %collective-permute-start.2) | collective-permute-done | bytes 262176 | tf_op jit(solution)/shard_map/ppermute | solution.py:15
  25.5 1.0 constant_dynamic-update-slice_fusion
  26.5 1.3 convert_bitcast_fusion
  27.8 0.6 copy.27
  28.4 0.0 copy-start.6
  28.4 112.7 %all_to_all.10 = bf16[2,64,8,2048]{3,2,0,1:T(8,128)(2,1)S(1)} all-to-all(bf16[2,64,8,2048]{3,2,0,1:T(8,128)(2,1)S(1)} %copy.27), channel_id=1, replica_groups=mesh['expert'=64,'tensor'=4] {'expert'}, dimensions={1} | all-to-all | bytes 8388608 | tf_op jit(solution)/shard_map/all_to_all | solution.py:68
  141.0 1.2 fusion.12
  142.3 1.9 copy-done.5
  144.2 1.3 fusion.5
  145.5 1.6 multiply_convert_fusion.2
  147.1 0.0 copy-start.7
  147.1 0.0 copy-start.9
  147.1 1.3 fusion.10
  148.4 3.3 %add_bitcast_fusion = f32[64,8,2048]{2,1,0:T(8,128)} fusion(f32[512,2048]{1,0:T(8,128)S(1)} %fusion.10, bf16[512,512]{1,0:T(8,128)(2,1)S(1)} %get-tuple-element.27, bf16[1,2048,512]{2,1,0:T(8,128)(2,1)S(1)} %copy-done), kind=kOutput, calls=%fused_computation | convolution fusion | flops 1074790400 | bytes 11010048 | tf_op jit(solution)/shard_map/dot_general | solution.py:101
  151.7 0.0 reduce-scatter.5.cloned.1.call-update
  151.7 0.2 reduce-scatter.3.cloned.1.call-start
  152.0 4.8 %fusion.3 = f32[64,8,2048]{2,1,0:T(8,128)} fusion(bf16[1,512,2048]{2,1,0:T(8,128)(2,1)} %param.15, bf16[512,512]{1,0:T(8,128)(2,1)S(1)} %get-tuple-element.25), kind=kOutput, calls=%fused_computation.12 | convolution fusion | flops 1073741824 | bytes 6815744 | tf_op jit(solution)/shard_map/dot_general | solution.py:82
  156.8 0.0 reduce-scatter.3.cloned.1.call-update
  156.8 38.6 %reduce-scatter.5.cloned.1.call-done = f32[64,8,512]{2,1,0:T(8,128)} async-done(((f32[64,8,2048]{2,1,0:T(8,128)}), f32[64,8,512]{2,1,0:T(8,128)}) %reduce-scatter.5.cloned.1.call-update) | async-done | bytes 1048592 | tf_op jit(solution)/shard_map/reduce_scatter | solution.py:106
  195.4 51.8 %reduce-scatter.3.cloned.1.call-done = f32[64,8,512]{2,1,0:T(8,128)} async-done(((f32[64,8,2048]{2,1,0:T(8,128)}), f32[64,8,512]{2,1,0:T(8,128)}) %reduce-scatter.3.cloned.1.call-update) | async-done | bytes 1048592 | tf_op jit(solution)/shard_map/reduce_scatter | solution.py:105
  247.3 2.8 broadcast_select_fusion
  250.1 0.7 collective-permute-start.3
  250.8 2.3 collective-permute-done.3
  253.1 0.4 add_convert_fusion
  253.5 1.0 copy.28
  254.5 10.4 %all-to-all-start.1 = ((bf16[2,64,4,512]{3,2,0,1:T(4,128)(2,1)}), bf16[2,64,4,512]{3,2,0,1:T(4,128)(2,1)S(1)}, u32[]{:S(2)}, u32[]{:S(2)}) async-start(bf16[2,64,4,512]{3,2,0,1:T(4,128)(2,1)} %copy.28), calls=%async_computation.3 | async-start | bytes 1048576 | tf_op jit(solution)/shard_map/all_to_all | solution.py:113
  264.9 0.0 copy-start.8
  264.9 4.5 %fusion.2 = bf16[1,512,2048]{2,1,0:T(8,128)(2,1)} fusion(bf16[512,512]{1,0:T(8,128)(2,1)} %copy-done.9, bf16[2,64,8,2048]{3,2,0,1:T(8,128)(2,1)} %copy-done.1), kind=kOutput, calls=%fused_computation.7 | convolution fusion | flops 1074790400 | bytes 4718592 | tf_op jit(solution)/shard_map/dot_general | solution.py:96
  269.4 2.6 fusion
  272.1 2.6 fusion.1
  274.7 7.5 %all-to-all-done.1 = bf16[2,64,4,512]{3,2,0,1:T(4,128)(2,1)S(1)} async-done(((bf16[2,64,4,512]{3,2,0,1:T(4,128)(2,1)}), bf16[2,64,4,512]{3,2,0,1:T(4,128)(2,1)S(1)}, u32[]{:S(2)}, u32[]{:S(2)}) %all-to-all-start.1) | async-done | bytes 524320 | tf_op jit(solution)/shard_map/all_to_all | solution.py:113
  282.2 0.4 copy.29
  282.6 0.4 fusion.14
  283.0 0.8 copy.31
  283.8 0.8 copy.32
  (25 shorter events, 0.1 us)
Async XLA Ops:
  7.2 138.3 %copy-start = (bf16[1,2048,512]{2,1,0:T(8,128)(2,1)S(1)}, bf16[1,2048,512]{2,1,0:T(8,128)(2,1)}, u32[]{:S(2)}) copy-start(bf16[1,2048,512]{2,1,0:T(8,128)(2,1)} %param.14) | copy-start | bytes 6291460
  7.2 7.0 %copy-start.12 = (s32[128,1]{0,1:T(1,128)S(1)}, s32[128,1]{0,1:T(1,128)}, u32[]{:S(2)}) copy-start(s32[128,1]{0,1:T(1,128)} %param.9) | copy-start | bytes 1540
  7.2 188.2 %reduce-scatter.5.cloned.1.call-start = ((), (), s32[]{:S(2)}) async-start(), calls=%async_computation.5 | async-start | bytes 5242880 | tf_op jit(solution)/shard_map/reduce_scatter | solution.py:106
  10.9 7.3 %collective-permute-start = (bf16[2,128,512]{2,1,0:T(8,128)(2,1)}, bf16[2,128,512]{2,1,0:T(8,128)(2,1)S(1)}, u32[]{:S(2)}, u32[]{:S(2)}) collective-permute-start(bf16[2,128,512]{2,1,0:T(8,128)(2,1)} %get-tuple-element.30), channel_id=1, source_target_pairs={{0,1},{1,2},{2,3},{3,0},{4,5},{5,6},{6,7},{7,4},{8,9},{9,10},{10,1... | collective-permute-start | bytes 786440 | tf_op jit(solution)/shard_map/ppermute | solution.py:15
  13.0 7.3 %collective-permute-start.1 = (bf16[2,128,512]{2,1,0:T(8,128)(2,1)}, bf16[2,128,512]{2,1,0:T(8,128)(2,1)}, u32[]{:S(2)}, u32[]{:S(2)}) collective-permute-start(bf16[2,128,512]{2,1,0:T(8,128)(2,1)} %get-tuple-element.30), channel_id=1, source_target_pairs={{0,3},{1,0},{2,1},{3,2},{4,7},{5,4},{6,5},{7,6},{8,11},{9,8},{10,9... | collective-permute-start | bytes 786440 | tf_op jit(solution)/shard_map/ppermute | solution.py:18
  18.2 7.3 %collective-permute-start.2 = (bf16[2,128,512]{2,1,0:T(8,128)(2,1)S(1)}, bf16[2,128,512]{2,1,0:T(8,128)(2,1)}, u32[]{:S(2)}, u32[]{:S(2)}) collective-permute-start(bf16[2,128,512]{2,1,0:T(8,128)(2,1)S(1)} %collective-permute-done), channel_id=1, source_target_pairs={{0,1},{1,2},{2,3},{3,0},{4,5},{5,6},{6,7},{7,4},{8,9},{9,10},{10,1... | collective-permute-start | bytes 786440 | tf_op jit(solution)/shard_map/ppermute | solution.py:15
  28.4 112.7 %copy-start.6 = (bf16[1,2048,512]{2,1,0:T(8,128)(2,1)S(1)}, bf16[1,2048,512]{2,1,0:T(8,128)(2,1)}, u32[]{:S(2)}) copy-start(bf16[1,2048,512]{2,1,0:T(8,128)(2,1)} %param.13) | copy-start | bytes 6291460
  141.0 4.4 %copy-start.1 = (bf16[2,64,8,2048]{3,2,0,1:T(8,128)(2,1)}, bf16[2,64,8,2048]{3,2,0,1:T(8,128)(2,1)S(1)}, u32[]{:S(2)}) copy-start(bf16[2,64,8,2048]{3,2,0,1:T(8,128)(2,1)S(1)} %all_to_all.10) | copy-start | bytes 12582916
  141.0 3.1 %copy-start.5 = (bf16[1,512,2048]{2,1,0:T(8,128)(2,1)S(1)}, bf16[1,512,2048]{2,1,0:T(8,128)(2,1)}, u32[]{:S(2)}) copy-start(bf16[1,512,2048]{2,1,0:T(8,128)(2,1)} %param.15) | copy-start | bytes 6291460
  147.1 1.3 copy-start.7
  147.1 1.3 copy-start.10
  147.1 4.8 %copy-start.9 = (bf16[512,512]{1,0:T(8,128)(2,1)}, bf16[512,512]{1,0:T(8,128)(2,1)S(1)}, u32[]{:S(2)}) copy-start(bf16[512,512]{1,0:T(8,128)(2,1)S(1)} %get-tuple-element.25) | copy-start | bytes 1572868
  151.7 95.5 %reduce-scatter.3.cloned.1.call-start = ((), (), s32[]{:S(2)}) async-start(), calls=%async_computation.4 | async-start | bytes 5242880 | tf_op jit(solution)/shard_map/reduce_scatter | solution.py:105
  195.4 57.7 %copy-start.3 = (f32[64,8,512]{2,1,0:T(8,128)S(1)}, f32[64,8,512]{2,1,0:T(8,128)}, u32[]{:S(2)}) copy-start(f32[64,8,512]{2,1,0:T(8,128)} %reduce-scatter.5.cloned.1.call-done) | copy-start | bytes 3145732
  247.3 5.8 %copy-start.4 = (f32[64,8,512]{2,1,0:T(8,128)S(1)}, f32[64,8,512]{2,1,0:T(8,128)}, u32[]{:S(2)}) copy-start(f32[64,8,512]{2,1,0:T(8,128)} %reduce-scatter.3.cloned.1.call-done) | copy-start | bytes 3145732
  250.1 3.0 %collective-permute-start.3 = (f32[2,64,4,512]{3,2,1,0:T(4,128)S(1)}, f32[2,64,4,512]{3,2,1,0:T(4,128)S(1)}, u32[]{:S(2)}, u32[]{:S(2)}) collective-permute-start(f32[2,64,4,512]{3,2,1,0:T(4,128)S(1)} %broadcast_select_fusion), channel_id=1, source_target_pairs={{0,4},{4,0},{8,12},{12,8},{16,20},{20,16},{24,28},{28,24},{32,36},... | collective-permute-start | bytes 3145736 | tf_op jit(solution)/shard_map/ppermute | solution.py:26
  254.5 27.7 %all-to-all-start.1 = ((bf16[2,64,4,512]{3,2,0,1:T(4,128)(2,1)}), bf16[2,64,4,512]{3,2,0,1:T(4,128)(2,1)S(1)}, u32[]{:S(2)}, u32[]{:S(2)}) async-start(bf16[2,64,4,512]{3,2,0,1:T(4,128)(2,1)} %copy.28), calls=%async_computation.3 | async-start | bytes 1048576 | tf_op jit(solution)/shard_map/all_to_all | solution.py:113
  264.9 4.5 %copy-start.2 = (bf16[2,64,8,2048]{3,2,0,1:T(8,128)(2,1)S(1)}, bf16[2,64,8,2048]{3,2,0,1:T(8,128)(2,1)}, u32[]{:S(2)}) copy-start(bf16[2,64,8,2048]{3,2,0,1:T(8,128)(2,1)} %copy-done.1) | copy-start | bytes 12582916
  264.9 4.5 %copy-start.8 = (bf16[512,512]{1,0:T(8,128)(2,1)S(1)}, bf16[512,512]{1,0:T(8,128)(2,1)}, u32[]{:S(2)}) copy-start(bf16[512,512]{1,0:T(8,128)(2,1)} %copy-done.7) | copy-start | bytes 1572868
  269.4 2.6 copy-start.11
Sparse Core Ops, SparseCore 0:
  151.9 43.5 reduce-scatter.4
  198.1 49.0 reduce-scatter.2
